TPU v7x, 512 devices: a whole 4x4x16 slice. The times are simulated.
512 devices in a mesh: col: 4 (over x_lo, core), gx: 16 (over z), gy: 8 (over x_hi, y).
Axes of the slice: x: 4 (x_hi: 2, x_lo: 2; x = x_hi * 2 + x_lo), y: 4, z: 16, core: 2. Of those that a mesh axis runs over, the one named last changes fastest.
Arguments:
- volume: float32 [32, 8, 64, 1024], P('col', None, 'gx', 'gy'), may hold values from -6 to 6
- filters: float32 [32, 32, 3, 3, 3], P('col'), may hold values from -0.21875 to 0.21875
- upstream: float32 [32, 8, 64, 1024], P('col', None, 'gx', 'gy'), may hold values from -6 to 6
Outputs:
- response: float32 [32, 8, 64, 1024], P('col', None, 'gx', 'gy')
- input_grad: float32 [32, 8, 64, 1024], P('col', None, 'gx', 'gy')
- filter_grad: float32 [32, 32, 3, 3, 3], P('col')
All inputs are finite; a program needn't handle non-finite values.
Results may differ from a plain program's by a relative error of at most 0.0003.
Values sent between devices are 32-bit elements; how exact they have to be, the bound alone decides.
No kernel may reach another device: no remote copies, remote signals or barrier semaphores. Data moves between devices by JAX's collectives and lax.ppermute only.
A program may use at most 64 MiB of HBM per device.

v0:
```python
import jax
import jax.numpy as jnp
from jax import lax
from jax.sharding import PartitionSpec as P


def with_halo(block, sides, width):
    for axis, dim in sides:
        count = lax.axis_size(axis)
        forward = [(i, i + 1) for i in range(count - 1)]
        backward = [(target, source) for source, target in forward]
        low = lax.ppermute(
            lax.slice_in_dim(block, block.shape[dim] - width, None, axis=dim), axis, forward
        )
        high = lax.ppermute(lax.slice_in_dim(block, 0, width, axis=dim), axis, backward)
        block = jnp.concatenate([low, block, high], axis=dim)
    return block


def pad_depth(field):
    return jnp.pad(field, ((0, 0), (1, 1), (0, 0), (0, 0)))


def forward_conv(padded, weights, planes, rows_x, rows_y):
    output = jnp.zeros((weights.shape[0], planes, rows_x, rows_y), jnp.float32)
    for depth in range(3):
        for across in range(3):
            for along in range(3):
                window = padded[
                    :, depth : depth + planes, across : across + rows_x, along : along + rows_y
                ]
                output = output + jnp.einsum(
                    "oc,czxy->ozxy",
                    weights[:, :, depth, across, along],
                    window,
                    precision=lax.Precision.HIGHEST,
                )
    return output


def backward_conv(padded_up, weights, planes, rows_x, rows_y):
    output = jnp.zeros((weights.shape[1], planes, rows_x, rows_y), jnp.float32)
    for depth in range(3):
        for across in range(3):
            for along in range(3):
                window = padded_up[
                    :,
                    2 - depth : 2 - depth + planes,
                    2 - across : 2 - across + rows_x,
                    2 - along : 2 - along + rows_y,
                ]
                output = output + jnp.einsum(
                    "oc,ozxy->czxy",
                    weights[:, :, depth, across, along],
                    window,
                    precision=lax.Precision.HIGHEST,
                )
    return output


def weight_terms(cotangent, padded, planes, rows_x, rows_y):
    pieces = []
    for depth in range(3):
        for across in range(3):
            for along in range(3):
                window = padded[
                    :, depth : depth + planes, across : across + rows_x, along : along + rows_y
                ]
                pieces.append(
                    jnp.einsum("ozxy,czxy->oc", cotangent, window, precision=lax.Precision.HIGHEST)
                )
    stacked = jnp.stack(pieces, axis=-1)
    return stacked.reshape(stacked.shape[0], stacked.shape[1], 3, 3, 3)


def shards(volume, filters, upstream):
    planes, rows_x, rows_y = (volume.shape[1], volume.shape[2], volume.shape[3])
    own_inputs = volume.shape[0]
    scale = (planes * rows_x * lax.axis_size("gx") * rows_y * lax.axis_size("gy")) ** (-0.5)
    gathered = lax.all_gather(volume, "col", axis=0, tiled=True)
    padded = pad_depth(with_halo(gathered, (("gx", 2), ("gy", 3)), 1))
    response = forward_conv(padded, filters, planes, rows_x, rows_y)
    all_rows = lax.all_gather(filters, "col", axis=0, tiled=True)
    all_upstream = lax.all_gather(upstream, "col", axis=0, tiled=True)
    padded_up = pad_depth(with_halo(all_upstream, (("gx", 2), ("gy", 3)), 1))
    first = lax.axis_index("col") * own_inputs
    own_filters = lax.dynamic_slice_in_dim(all_rows, first, own_inputs, 1)
    input_grad = backward_conv(padded_up, own_filters, planes, rows_x, rows_y)
    local_grad = weight_terms(upstream, padded, planes, rows_x, rows_y)
    total_grad = lax.psum(local_grad, ("gx", "gy"))
    return (response, input_grad, total_grad * scale)


def solution(mesh):
    placed = (
        P("col", None, "gx", "gy"),
        P("col", None, None, None, None),
        P("col", None, "gx", "gy"),
    )
    return jax.shard_map(
        shards,
        mesh=mesh,
        in_specs=placed,
        out_specs=(
            P("col", None, "gx", "gy"),
            P("col", None, "gx", "gy"),
            P("col", None, None, None, None),
        ),
        check_vma=False,
    )
```

profile of v0, /device:TPU:2, one launch (start us, length us, event | category | flops | bytes accessed | tf_op | source)
XLA Modules:
  0.0 888.0 jit_solution(7384138758110080891)
XLA Ops:
  1.7 11.6 %all_gather.9 = f32[32,8,4,128]{3,0,2,1:T(8,128)S(1)} all-gather(f32[8,8,4,128]{3,0,2,1:T(8,128)S(1)} %copy.65), channel_id=1, replica_groups=mesh['col'=4,'gx'=16,'gy'=8] {'col'}, dimensions={0}, use_global_device_ids=true | all-gather | bytes 655360 | tf_op jit(solution)/shard_map/all_gather | solution.py:80
  17.5 7.3 all_gather.11
  25.5 4.9 collective-permute-start.4
  31.7 6.6 all_gather.10
  41.8 1.9 collective-permute-start.2
  49.1 2.1 copy.74
  51.1 5.1 collective-permute-start.6
  60.5 2.0 fusion.116
  62.6 2.0 fusion.112
  67.8 2.9 pad_maximum_fusion.9
  70.7 2.1 select_maximum_fusion.2
  73.9 2.0 copy.77
  75.9 1.9 select_maximum_fusion
  104.6 4.3 fusion.309
  108.8 1.8 fusion.212
  110.7 1.8 fusion.214
  114.2 1.8 fusion.218
  116.1 1.8 fusion.220
  119.6 1.9 fusion.224
  121.5 1.9 fusion.226
  125.2 1.9 convolution_bitcast_fusion.7
  127.1 1.9 convolution_bitcast_fusion.8
  153.7 715.1 %psum.7 = f32[8,32,3,3,3]{1,0,4,3,2:T(8,128)} all-reduce(f32[8,32,3,3,3]{1,0,4,3,2:T(8,128)} %bitcast.738), channel_id=1, replica_groups=mesh['col'=4,'gx'=16,'gy'=8] {'gx','gy'}, use_global_device_ids=true, to_apply=%region_0.1 | all-reduce | flops 6912 | bytes 55296 | tf_op jit(solution)/shard_map/psum | solution.py:90
  870.6 2.3 fusion.48
  (238 shorter events, 97.4 us)
Async XLA Ops:
  0.6 31.1 %copy-start.65 = (f32[8,32,3,3,3]{1,0,4,3,2:T(8,128)S(1)}, f32[8,32,3,3,3]{1,0,4,3,2:T(8,128)}, u32[]{:S(2)}) copy-start(f32[8,32,3,3,3]{1,0,4,3,2:T(8,128)} %param.4) | copy-start | bytes 82948
  13.2 26.4 %copy-start.3 = (f32[32,8,4,128]{3,0,2,1:T(8,128)}, f32[32,8,4,128]{3,0,2,1:T(8,128)S(1)}, u32[]{:S(2)}) copy-start(f32[32,8,4,128]{3,0,2,1:T(8,128)S(1)} %all_gather.9) | copy-start | bytes 1572868
  13.9 25.5 %collective-permute-start = (f32[32,8,1,128]{3,0,2,1:T(8,128)S(1)}, f32[32,8,1,128]{3,0,2,1:T(8,128)S(1)}, u32[]{:S(2)}, u32[]{:S(2)}) collective-permute-start(f32[32,8,1,128]{3,0,2,1:T(8,128)S(1)} %get-tuple-element.46), channel_id=1, source_target_pairs={{0,8},{8,16},{16,24},{24,32},{32,40},{40,48},{48,56},{56,64},{64,7... | collective-permute-start | bytes 393224 | tf_op jit(solution)/shard_map/ppermute | solution.py:12
  15.2 24.4 %collective-permute-start.1 = (f32[32,8,1,128]{3,0,2,1:T(8,128)}, f32[32,8,1,128]{3,0,2,1:T(8,128)S(1)}, u32[]{:S(2)}, u32[]{:S(2)}) collective-permute-start(f32[32,8,1,128]{3,0,2,1:T(8,128)} %get-tuple-element.45), channel_id=1, source_target_pairs={{8,0},{16,8},{24,16},{32,24},{40,32},{48,40},{56,48},{64,56},{72,6... | collective-permute-start | bytes 393224 | tf_op jit(solution)/shard_map/ppermute | solution.py:15
  25.5 20.4 %collective-permute-start.4 = (f32[32,8,1,128]{3,0,2,1:T(8,128)}, f32[32,8,1,128]{3,0,2,1:T(8,128)}, u32[]{:S(2)}, u32[]{:S(2)}) collective-permute-start(f32[32,8,1,128]{3,0,2,1:T(8,128)} %get-tuple-element.41), channel_id=1, source_target_pairs={{0,8},{8,16},{16,24},{24,32},{32,40},{40,48},{48,56},{56,64},{64,7... | collective-permute-start | bytes 393224 | tf_op jit(solution)/shard_map/ppermute | solution.py:12
  30.4 16.4 %collective-permute-start.5 = (f32[32,8,1,128]{3,0,2,1:T(8,128)}, f32[32,8,1,128]{3,0,2,1:T(8,128)}, u32[]{:S(2)}, u32[]{:S(2)}) collective-permute-start(f32[32,8,1,128]{3,0,2,1:T(8,128)} %get-tuple-element.40), channel_id=1, source_target_pairs={{8,0},{16,8},{24,16},{32,24},{40,32},{48,40},{56,48},{64,56},{72,6... | collective-permute-start | bytes 393224 | tf_op jit(solution)/shard_map/ppermute | solution.py:15
  41.8 22.8 %collective-permute-start.2 = (f32[32,8,6,1]{0,1,3,2:T(8,128)}, f32[32,8,6,1]{0,1,3,2:T(8,128)}, u32[]{:S(2)}, u32[]{:S(2)}) collective-permute-start(f32[32,8,6,1]{0,1,3,2:T(8,128)} %copy.66), channel_id=1, source_target_pairs={{0,1},{1,2},{2,3},{3,4},{4,5},{5,6},{6,7},{8,9},{9,10},{10,11},{11... | collective-permute-start | bytes 18440 | tf_op jit(solution)/shard_map/ppermute | solution.py:12
  44.6 21.1 %collective-permute-start.3 = (f32[32,8,6,1]{0,1,3,2:T(8,128)}, f32[32,8,6,1]{0,1,3,2:T(8,128)}, u32[]{:S(2)}, u32[]{:S(2)}) collective-permute-start(f32[32,8,6,1]{0,1,3,2:T(8,128)} %copy.67), channel_id=1, source_target_pairs={{1,0},{2,1},{3,2},{4,3},{5,4},{6,5},{7,6},{9,8},{10,9},{11,10},{12... | collective-permute-start | bytes 18440 | tf_op jit(solution)/shard_map/ppermute | solution.py:15
  47.8 11.0 %copy-start.20 = (f32[32,8,5,128]{3,0,2,1:T(8,128)S(1)}, f32[32,8,5,128]{3,0,2,1:T(8,128)}, u32[]{:S(2)}) copy-start(f32[32,8,5,128]{3,0,2,1:T(8,128)} %copy-done.19) | copy-start | bytes 1966084
  51.1 21.6 %collective-permute-start.6 = (f32[32,8,6,1]{0,1,3,2:T(8,128)}, f32[32,8,6,1]{0,1,3,2:T(8,128)}, u32[]{:S(2)}, u32[]{:S(2)}) collective-permute-start(f32[32,8,6,1]{0,1,3,2:T(8,128)} %copy.74), channel_id=1, source_target_pairs={{0,1},{1,2},{2,3},{3,4},{4,5},{5,6},{6,7},{8,9},{9,10},{10,11},{11... | collective-permute-start | bytes 18440 | tf_op jit(solution)/shard_map/ppermute | solution.py:12
  57.2 16.7 %collective-permute-start.7 = (f32[32,8,6,1]{0,1,3,2:T(8,128)}, f32[32,8,6,1]{0,1,3,2:T(8,128)}, u32[]{:S(2)}, u32[]{:S(2)}) collective-permute-start(f32[32,8,6,1]{0,1,3,2:T(8,128)} %copy.75), channel_id=1, source_target_pairs={{1,0},{2,1},{3,2},{4,3},{5,4},{6,5},{7,6},{9,8},{10,9},{11,10},{12... | collective-permute-start | bytes 18440 | tf_op jit(solution)/shard_map/ppermute | solution.py:15
  77.7 22.6 %copy-start.1 = (f32[32,10,6,130]{3,0,2,1:T(8,128)}, f32[32,10,6,130]{3,0,2,1:T(8,128)S(1)}, u32[]{:S(2)}) copy-start(f32[32,10,6,130]{3,0,2,1:T(8,128)S(1)} %select_maximum_fusion) | copy-start | bytes 2995204
  119.6 11.2 %copy-start = (f32[8,8,4,128]{3,2,1,0:T(4,128)S(1)}, f32[8,8,4,128]{3,2,1,0:T(4,128)}, u32[]{:S(2)}) copy-start(f32[8,8,4,128]{3,2,1,0:T(4,128)} %param.5) | copy-start | bytes 393220
  119.6 11.2 %copy-start.33 = (f32[32,8,4,128]{3,0,2,1:T(8,128)S(1)}, f32[32,8,4,128]{3,0,2,1:T(8,128)}, u32[]{:S(2)}) copy-start(f32[32,8,4,128]{3,0,2,1:T(8,128)} %get-tuple-element.26) | copy-start | bytes 1572868
  121.5 9.8 %copy-start.13 = (f32[32,8,4,128]{3,0,2,1:T(8,128)S(1)}, f32[32,8,4,128]{3,0,2,1:T(8,128)}, u32[]{:S(2)}) copy-start(f32[32,8,4,128]{3,0,2,1:T(8,128)} %get-tuple-element.28) | copy-start | bytes 1572868
  123.4 9.7 %copy-start.32 = (f32[32,8,4,128]{3,0,2,1:T(8,128)S(1)}, f32[32,8,4,128]{3,0,2,1:T(8,128)}, u32[]{:S(2)}) copy-start(f32[32,8,4,128]{3,0,2,1:T(8,128)} %get-tuple-element.25) | copy-start | bytes 1572868
  125.2 8.5 copy-start.31
  127.1 7.1 copy-start.30
  129.0 5.8 copy-start.29
  137.5 6.0 copy-start.4
  138.1 5.9 copy-start.10
  138.8 7.0 copy-start.14
  140.6 5.8 copy-start.8
  141.1 5.8 copy-start.17
  (51 other events, 165.5 us)
where the time goes:
time: 893 us; the launch traced here: 888 us
  blocking collectives  741 us (83%)
  matrix products  92.9 us (10%)
  local copies, waits for them, and re-layouts  25.6 us (3%)
  starting transfers between devices  18.6 us (2%)
    psum x1, blocking collectives, shards(): total_grad = lax.psum(local_grad, ('gx', 'gy'))  715 us
    dot_general x27, matrix products, forward_conv(): jnp.einsum('oc,czxy->ozxy', weights[:, :, depth, across, along], window,...  42.3 us
    dot_general x27, matrix products, backward_conv(): jnp.einsum('oc,ozxy->czxy', weights[:, :, depth, across, along], window,...  35.7 us
  transfers between devices with their start and end apart: 8, of which 0 were waited for; matrix products, arithmetic and copies ran while one was open for 3% of the time, Pallas kernels for 0%

commit v1 on v0

--- a/solution.py
+++ b/solution.py
@@ -87,7 +87,7 @@
     own_filters = lax.dynamic_slice_in_dim(all_rows, first, own_inputs, 1)
     input_grad = backward_conv(padded_up, own_filters, planes, rows_x, rows_y)
     local_grad = weight_terms(upstream, padded, planes, rows_x, rows_y)
-    total_grad = lax.psum(local_grad, ("gx", "gy"))
+    total_grad = jnp.sum(lax.all_gather(local_grad, ("gx", "gy")), axis=0)
     return (response, input_grad, total_grad * scale)
 
 

time: 893 us -> 432 us (0.48)
  the two profiles are of different devices: /device:TPU:2 before, /device:TPU:8 now
where the time goes in v1:
time: 432 us; the launch traced here: 428 us
  waiting for transfers between devices  263 us (61%)
  matrix products  67.1 us (16%)
  starting transfers between devices  28.1 us (7%)
  local copies, waits for them, and re-layouts  21.8 us (5%)
  blocking collectives  20.4 us (5%)
  between operations  15.4 us (4%)
  other arithmetic  12 us (3%)
    all_gather x1, waiting for transfers between devices, shards(): total_grad = jnp.sum(lax.all_gather(local_grad, ('gx', 'gy')), axis=0)  263 us
    dot_general x27, matrix products, backward_conv(): jnp.einsum('oc,ozxy->czxy', weights[:, :, depth, across, along], window,...  35.6 us
    dot_general x27, matrix products, weight_terms(): jnp.einsum('ozxy,czxy->oc', cotangent, window, precision=lax.Precision.HI...  18.3 us
    ppermute x4, starting transfers between devices, with_halo(): lax.ppermute(lax.slice_in_dim(block, block.shape[dim] - width, None, axis...  14.1 us
    ppermute x4, starting transfers between devices, with_halo(): lax.ppermute(lax.slice_in_dim(block, 0, width, axis=dim), axis, backward)  14 us
    dot_general x27, matrix products, forward_conv(): jnp.einsum('oc,czxy->ozxy', weights[:, :, depth, across, along], window,...  13.2 us
  transfers between devices with their start and end apart: 9, of which 1 were waited for; matrix products, arithmetic and copies ran while one was open for 14% of the time, Pallas kernels for 0%

profile of v1, /device:TPU:8, one launch (start us, length us, event | category | flops | bytes accessed | tf_op | source)
XLA Modules:
  0.0 428.1 jit_solution(17874844922462230376)
XLA Ops:
  8.2 7.2 %all_gather.14 = f32[32,8,4,128]{3,0,2,1:T(8,128)S(1)} all-gather(f32[8,8,4,128]{3,0,2,1:T(8,128)S(1)} %copy.73), channel_id=1, replica_groups=mesh['col'=4,'gx'=16,'gy'=8] {'col'}, dimensions={0}, use_global_device_ids=true | all-gather | bytes 655360 | tf_op jit(solution)/shard_map/all_gather | solution.py:84
  17.4 5.2 %collective-permute-start.4 = (f32[32,8,1,128]{3,0,2,1:T(8,128)}, f32[32,8,1,128]{3,0,2,1:T(8,128)}, u32[]{:S(2)}, u32[]{:S(2)}) collective-permute-start(f32[32,8,1,128]{3,0,2,1:T(8,128)} %get-tuple-element.41), channel_id=1, source_target_pairs={{0,8},{8,16},{16,24},{24,32},{32,40},{40,48},{48,56},{56,64},{64,7... | collective-permute-start | bytes 393224 | tf_op jit(solution)/shard_map/ppermute | solution.py:12
  23.6 6.9 %all_gather.12 = f32[32,8,4,128]{3,0,2,1:T(8,128)S(1)} all-gather(f32[8,8,4,128]{3,0,2,1:T(8,128)S(1)} %copy.65), channel_id=1, replica_groups=mesh['col'=4,'gx'=16,'gy'=8] {'col'}, dimensions={0}, use_global_device_ids=true | all-gather | bytes 655360 | tf_op jit(solution)/shard_map/all_gather | solution.py:80
  31.8 4.6 %collective-permute-start = (f32[32,8,1,128]{3,0,2,1:T(8,128)S(1)}, f32[32,8,1,128]{3,0,2,1:T(8,128)S(1)}, u32[]{:S(2)}, u32[]{:S(2)}) collective-permute-start(f32[32,8,1,128]{3,0,2,1:T(8,128)S(1)} %get-tuple-element.46), channel_id=1, source_target_pairs={{0,8},{8,16},{16,24},{24,32},{32,40},{40,48},{48,56},{56,64},{64,7... | collective-permute-start | bytes 393224 | tf_op jit(solution)/shard_map/ppermute | solution.py:12
  36.4 6.3 %all_gather.13 = f32[32,32,3,3,3]{1,0,4,3,2:T(8,128)S(1)} all-gather(f32[8,32,3,3,3]{1,0,4,3,2:T(8,128)S(1)} %copy-done.68), channel_id=1, replica_groups=mesh['col'=4,'gx'=16,'gy'=8] {'col'}, dimensions={0}, use_global_device_ids=true | all-gather | bytes 138240 | tf_op jit(solution)/shard_map/all_gather | solution.py:83
  47.2 7.0 %collective-permute-start.3 = (f32[32,8,6,1]{0,1,3,2:T(8,128)}, f32[32,8,6,1]{0,1,3,2:T(8,128)}, u32[]{:S(2)}, u32[]{:S(2)}) collective-permute-start(f32[32,8,6,1]{0,1,3,2:T(8,128)} %copy.67), channel_id=1, source_target_pairs={{1,0},{2,1},{3,2},{4,3},{5,4},{6,5},{7,6},{9,8},{10,9},{11,10},{12... | collective-permute-start | bytes 18440 | tf_op jit(solution)/shard_map/ppermute | solution.py:15
  54.2 1.9 collective-permute-start.2
  56.1 1.7 fusion.208
  61.4 4.5 %collective-permute-start.7 = (f32[32,8,6,1]{0,1,3,2:T(8,128)S(1)}, f32[32,8,6,1]{0,1,3,2:T(8,128)S(1)}, u32[]{:S(2)}, u32[]{:S(2)}) collective-permute-start(f32[32,8,6,1]{0,1,3,2:T(8,128)S(1)} %copy.75), channel_id=1, source_target_pairs={{1,0},{2,1},{3,2},{4,3},{5,4},{6,5},{7,6},{9,8},{10,9},{11,10},{12... | collective-permute-start | bytes 18440 | tf_op jit(solution)/shard_map/ppermute | solution.py:15
  65.9 2.4 collective-permute-start.6
  68.3 2.0 fusion.116
  70.3 2.0 fusion.112
  97.4 2.0 copy.68
  99.4 2.0 copy.69
  101.4 2.4 select_maximum_fusion.2
  103.9 2.3 pad_maximum_fusion.9
  106.1 5.3 %fusion.309 = (f32[32,8,4,128]{3,0,2,1:T(8,128)}, f32[32,8,4,128]{3,0,2,1:T(8,128)}, f32[32,8,4,128]{3,0,2,1:T(8,128)}, f32[32,8,4,128]{3,0,2,1:T(8,128)}, f32[3...) fusion(f32[32,10,6,130]{3,0,2,1:T(8,128)S(1)} %select_maximum_f, ...), kind=kLoop, calls=%fused_computation.415 | loop fusion | bytes 18874368 | tf_op jit(solution)/shard_map/slice | solution.py:29
  111.5 1.7 fusion.76
  113.2 1.7 fusion.75
  114.9 1.7 fusion.74
  130.8 2.1 fusion.83
  134.6 1.8 fusion.48
  151.2 263.2 %all-gather.2.cloned.1.call-done = f32[128,8,32,3,3,3]{2,1,5,4,3,0:T(8,128)} async-done(((f32[1,8,32,3,3,3]{2,1,5,4,3,0:T(8,128)}), f32[128,8,32,3,3,3]{2,1,5,4,3,0:T(8,128)}) %all-gather.2.cloned.1.call-update) | async-done | bytes 3538960 | tf_op jit(solution)/shard_map/all_gather | solution.py:90
  414.4 6.0 %reduce_sum.9 = f32[8,32,3,3,3]{1,0,4,3,2:T(8,128)S(1)} reduce(f32[128,8,32,3,3,3]{2,1,5,4,3,0:T(8,128)} %all-gather.2.cloned.1.call-done, f32[]{:T(128)} %constant.3.clone.1), dimensions={0}, to_apply=%region_0.1 | reduce | flops 877824 | bytes 3566596 | tf_op jit(solution)/shard_map/reduce_sum | solution.py:90
  (249 shorter events, 68.9 us)
Async XLA Ops:
  7.2 29.2 %copy-start.68 = (f32[8,32,3,3,3]{1,0,4,3,2:T(8,128)S(1)}, f32[8,32,3,3,3]{1,0,4,3,2:T(8,128)}, u32[]{:S(2)}) copy-start(f32[8,32,3,3,3]{1,0,4,3,2:T(8,128)} %param.4) | copy-start | bytes 82948
  7.2 407.2 %all-gather.2.cloned.1.call-start = ((), (), s32[]{:S(2)}) async-start(), calls=%async_computation | async-start | bytes 14266368 | tf_op jit(solution)/shard_map/all_gather | solution.py:90
  16.1 42.7 %collective-permute-start.5 = (f32[32,8,1,128]{3,0,2,1:T(8,128)}, f32[32,8,1,128]{3,0,2,1:T(8,128)}, u32[]{:S(2)}, u32[]{:S(2)}) collective-permute-start(f32[32,8,1,128]{3,0,2,1:T(8,128)} %get-tuple-element.40), channel_id=1, source_target_pairs={{8,0},{16,8},{24,16},{32,24},{40,32},{48,40},{56,48},{64,56},{72,6... | collective-permute-start | bytes 393224 | tf_op jit(solution)/shard_map/ppermute | solution.py:15
  17.4 40.5 %collective-permute-start.4 = (f32[32,8,1,128]{3,0,2,1:T(8,128)}, f32[32,8,1,128]{3,0,2,1:T(8,128)}, u32[]{:S(2)}, u32[]{:S(2)}) collective-permute-start(f32[32,8,1,128]{3,0,2,1:T(8,128)} %get-tuple-element.41), channel_id=1, source_target_pairs={{0,8},{8,16},{16,24},{24,32},{32,40},{40,48},{48,56},{56,64},{64,7... | collective-permute-start | bytes 393224 | tf_op jit(solution)/shard_map/ppermute | solution.py:12
  30.5 13.6 %copy-start.6 = (f32[32,8,4,128]{3,0,2,1:T(8,128)}, f32[32,8,4,128]{3,0,2,1:T(8,128)S(1)}, u32[]{:S(2)}) copy-start(f32[32,8,4,128]{3,0,2,1:T(8,128)S(1)} %all_gather.12) | copy-start | bytes 1572868
  30.5 13.6 %collective-permute-start.1 = (f32[32,8,1,128]{3,0,2,1:T(8,128)S(1)}, f32[32,8,1,128]{3,0,2,1:T(8,128)S(1)}, u32[]{:S(2)}, u32[]{:S(2)}) collective-permute-start(f32[32,8,1,128]{3,0,2,1:T(8,128)S(1)} %get-tuple-element.45), channel_id=1, source_target_pairs={{8,0},{16,8},{24,16},{32,24},{40,32},{48,40},{56,48},{64,56},{72,6... | collective-permute-start | bytes 393224 | tf_op jit(solution)/shard_map/ppermute | solution.py:15
  31.8 12.0 %collective-permute-start = (f32[32,8,1,128]{3,0,2,1:T(8,128)S(1)}, f32[32,8,1,128]{3,0,2,1:T(8,128)S(1)}, u32[]{:S(2)}, u32[]{:S(2)}) collective-permute-start(f32[32,8,1,128]{3,0,2,1:T(8,128)S(1)} %get-tuple-element.46), channel_id=1, source_target_pairs={{0,8},{8,16},{16,24},{24,32},{32,40},{40,48},{48,56},{56,64},{64,7... | collective-permute-start | bytes 393224 | tf_op jit(solution)/shard_map/ppermute | solution.py:12
  44.1 17.3 %copy-start.26 = (f32[32,8,5,128]{3,0,2,1:T(8,128)}, f32[32,8,5,128]{3,0,2,1:T(8,128)S(1)}, u32[]{:S(2)}) copy-start(f32[32,8,5,128]{3,0,2,1:T(8,128)S(1)} %get-tuple-element.43) | copy-start | bytes 1966084
  47.2 52.2 %collective-permute-start.3 = (f32[32,8,6,1]{0,1,3,2:T(8,128)}, f32[32,8,6,1]{0,1,3,2:T(8,128)}, u32[]{:S(2)}, u32[]{:S(2)}) collective-permute-start(f32[32,8,6,1]{0,1,3,2:T(8,128)} %copy.67), channel_id=1, source_target_pairs={{1,0},{2,1},{3,2},{4,3},{5,4},{6,5},{7,6},{9,8},{10,9},{11,10},{12... | collective-permute-start | bytes 18440 | tf_op jit(solution)/shard_map/ppermute | solution.py:15
  54.2 43.2 %collective-permute-start.2 = (f32[32,8,6,1]{0,1,3,2:T(8,128)}, f32[32,8,6,1]{0,1,3,2:T(8,128)}, u32[]{:S(2)}, u32[]{:S(2)}) collective-permute-start(f32[32,8,6,1]{0,1,3,2:T(8,128)} %copy.66), channel_id=1, source_target_pairs={{0,1},{1,2},{2,3},{3,4},{4,5},{5,6},{6,7},{8,9},{9,10},{10,11},{11... | collective-permute-start | bytes 18440 | tf_op jit(solution)/shard_map/ppermute | solution.py:12
  61.0 11.7 %copy-start.43 = (f32[32,32,3,3,3]{1,0,4,3,2:T(8,128)S(1)}, f32[32,32,3,3,3]{1,0,4,3,2:T(8,128)}, u32[]{:S(2)}) copy-start(f32[32,32,3,3,3]{1,0,4,3,2:T(8,128)} %copy-done.42) | copy-start | bytes 331780
  61.4 13.8 %collective-permute-start.7 = (f32[32,8,6,1]{0,1,3,2:T(8,128)S(1)}, f32[32,8,6,1]{0,1,3,2:T(8,128)S(1)}, u32[]{:S(2)}, u32[]{:S(2)}) collective-permute-start(f32[32,8,6,1]{0,1,3,2:T(8,128)S(1)} %copy.75), channel_id=1, source_target_pairs={{1,0},{2,1},{3,2},{4,3},{5,4},{6,5},{7,6},{9,8},{10,9},{11,10},{12... | collective-permute-start | bytes 18440 | tf_op jit(solution)/shard_map/ppermute | solution.py:15
  65.9 6.5 %collective-permute-start.6 = (f32[32,8,6,1]{0,1,3,2:T(8,128)}, f32[32,8,6,1]{0,1,3,2:T(8,128)S(1)}, u32[]{:S(2)}, u32[]{:S(2)}) collective-permute-start(f32[32,8,6,1]{0,1,3,2:T(8,128)} %copy.74), channel_id=1, source_target_pairs={{0,1},{1,2},{2,3},{3,4},{4,5},{5,6},{6,7},{8,9},{9,10},{10,11},{11... | collective-permute-start | bytes 18440 | tf_op jit(solution)/shard_map/ppermute | solution.py:12
  75.5 20.6 %copy-start.2 = (f32[32,8,6,1]{3,0,2,1:T(8,128)}, f32[32,8,6,1]{3,0,2,1:T(8,128)S(1)}, u32[]{:S(2)}) copy-start(f32[32,8,6,1]{3,0,2,1:T(8,128)S(1)} %copy.77) | copy-start | bytes 18436
  76.2 18.8 %copy-start.1 = (f32[32,10,6,130]{3,0,2,1:T(8,128)}, f32[32,10,6,130]{3,0,2,1:T(8,128)S(1)}, u32[]{:S(2)}) copy-start(f32[32,10,6,130]{3,0,2,1:T(8,128)S(1)} %select_maximum_fusion) | copy-start | bytes 2995204
  106.1 14.9 %copy-start.13 = (f32[32,8,4,128]{3,0,2,1:T(8,128)}, f32[32,8,4,128]{3,0,2,1:T(8,128)S(1)}, u32[]{:S(2)}) copy-start(f32[32,8,4,128]{3,0,2,1:T(8,128)S(1)} %get-tuple-element.36) | copy-start | bytes 1572868
  106.1 15.5 %copy-start.17 = (f32[32,8,4,128]{3,0,2,1:T(8,128)}, f32[32,8,4,128]{3,0,2,1:T(8,128)S(1)}, u32[]{:S(2)}) copy-start(f32[32,8,4,128]{3,0,2,1:T(8,128)S(1)} %get-tuple-element.29) | copy-start | bytes 1572868
  106.1 17.1 %copy-start.11 = (f32[32,8,4,128]{3,0,2,1:T(8,128)}, f32[32,8,4,128]{3,0,2,1:T(8,128)S(1)}, u32[]{:S(2)}) copy-start(f32[32,8,4,128]{3,0,2,1:T(8,128)S(1)} %get-tuple-element.27) | copy-start | bytes 1572868
  106.1 18.2 %copy-start.15 = (f32[32,8,4,128]{3,0,2,1:T(8,128)}, f32[32,8,4,128]{3,0,2,1:T(8,128)S(1)}, u32[]{:S(2)}) copy-start(f32[32,8,4,128]{3,0,2,1:T(8,128)S(1)} %get-tuple-element.35) | copy-start | bytes 1572868
  106.1 5.4 %copy-start = (f32[8,8,4,128]{3,2,1,0:T(4,128)S(1)}, f32[8,8,4,128]{3,2,1,0:T(4,128)}, u32[]{:S(2)}) copy-start(f32[8,8,4,128]{3,2,1,0:T(4,128)} %param.5) | copy-start | bytes 393220
  111.5 5.1 %copy-start.41 = (f32[32,8,4,128]{3,0,2,1:T(8,128)S(1)}, f32[32,8,4,128]{3,0,2,1:T(8,128)}, u32[]{:S(2)}) copy-start(f32[32,8,4,128]{3,0,2,1:T(8,128)} %get-tuple-element.23) | copy-start | bytes 1572868
  111.5 5.6 %copy-start.40 = (f32[32,8,4,128]{3,0,2,1:T(8,128)S(1)}, f32[32,8,4,128]{3,0,2,1:T(8,128)}, u32[]{:S(2)}) copy-start(f32[32,8,4,128]{3,0,2,1:T(8,128)} %get-tuple-element.22) | copy-start | bytes 1572868
  111.5 6.2 %copy-start.39 = (f32[32,8,4,128]{3,0,2,1:T(8,128)S(1)}, f32[32,8,4,128]{3,0,2,1:T(8,128)}, u32[]{:S(2)}) copy-start(f32[32,8,4,128]{3,0,2,1:T(8,128)} %get-tuple-element.21) | copy-start | bytes 1572868
  113.2 5.6 %copy-start.38 = (f32[32,8,4,128]{3,0,2,1:T(8,128)S(1)}, f32[32,8,4,128]{3,0,2,1:T(8,128)}, u32[]{:S(2)}) copy-start(f32[32,8,4,128]{3,0,2,1:T(8,128)} %get-tuple-element.19) | copy-start | bytes 1572868
  (56 other events, 172.7 us)
Sparse Core Ops, SparseCore 0:
  130.8 283.5 all-gather.1
